TPU v7x, 512 devices: a whole 4x4x16 slice. The times are simulated.
512 devices in a mesh: half: 2 (over core), cls: 64 (over z, x), vol: 4 (over y).
Axes of the slice: x: 4, y: 4, z: 16, core: 2. Of those that a mesh axis runs over, the one named last changes fastest.
Arguments:
- images: bfloat16 [16384, 16384], P(('half', 'cls'), 'vol')
- groups: int32 [16384, 1], P(('half', 'cls')), may hold values from 0 to 63; in each aligned block of 128 rows (0 to 127, 128 to 255, ...) at most 4 rows name the same one
- references: bfloat16 [2048, 16384], P('cls', 'vol'), may hold values from -0.046875 to 0.046875
- interp_index: int32 [2048, 16384], P('cls', 'vol'), may hold values from 0 to 2047
- shell_index: int32 [4, 262144], P('vol', ('half', 'cls')), may hold values from 0 to 127
Outputs:
- volume: float32 [4, 262144], P('vol', ('half', 'cls'))
- shell_fsc: float32 [128], replicated
Inputs may be any that keep to these rules, and one draw needn't show every extreme that they name: `groups`: within each aligned block of 128 particles no group appears more than 4 times, a bound that some block reaches.
All inputs are finite; a program needn't handle non-finite values.
Results may differ from a plain program's by a relative error of at most 0.00041.
Values may be sent and summed in bfloat16 or wider, within the bound.
No kernel may reach another device: no remote copies, remote signals or barrier semaphores. Data moves between devices by JAX's collectives and lax.ppermute only.
A program may use at most 64 MiB of HBM per device.

v0:
```python
import jax
import jax.numpy as jnp
from jax import lax
from jax.sharding import PartitionSpec as P

IMG = 128
SHIFTS = 5
NSHELL = 128
PLANES = 4
VBOX = 256
VOXS = 262144
EPS_W = 1e-05
EPS_F = 1e-06


def partner(shard, axis, apart):
    return lax.ppermute(shard, axis, [(i, i ^ 1 << apart) for i in range(lax.axis_size(axis))])


def shards(images, groups, references, interp_index, shell_index):
    n_cls = lax.axis_size("cls")
    n_vol = lax.axis_size("vol")
    n_half = lax.axis_size("half")
    part_count, pix_quarter = images.shape
    class_count = references.shape[0]
    capacity = max(2 * part_count // n_cls, 4)
    slot_count = n_cls * capacity
    owner_ids = groups[:, 0]
    matches = (owner_ids[:, None] == jnp.arange(n_cls, dtype=jnp.int32)[None, :]).astype(jnp.int32)
    order_in = jnp.sum(jnp.cumsum(matches, axis=0) * matches, axis=1) - 1
    slot_ids = owner_ids * capacity + order_in
    slot_hits = slot_ids[None, :] == jnp.arange(slot_count, dtype=jnp.int32)[:, None]
    source_ids = jnp.sum(
        jnp.where(slot_hits, jnp.arange(part_count, dtype=jnp.int32)[None, :], 0), axis=1
    )
    filled = jnp.any(slot_hits, axis=1)
    outgoing = jnp.where(
        filled[:, None], jnp.take(images, source_ids, axis=0), jnp.zeros((), jnp.bfloat16)
    )
    arrived = lax.all_to_all(
        outgoing.reshape(n_cls, capacity, pix_quarter),
        "cls",
        split_axis=0,
        concat_axis=0,
        tiled=True,
    )
    arrived = arrived.reshape(slot_count, pix_quarter)
    quarter_rows = pix_quarter // IMG
    shaped_refs = references.reshape(class_count, quarter_rows, IMG)
    rolled_refs = jnp.concatenate(
        [
            jnp.roll(shaped_refs, -(shift_id - SHIFTS // 2), axis=2).reshape(
                class_count, pix_quarter
            )
            for shift_id in range(SHIFTS)
        ],
        axis=0,
    )
    partial_scores = lax.dot_general(
        arrived, rolled_refs, (((1,), (1,)), ((), ())), preferred_element_type=jnp.float32
    )
    partial_scores = partial_scores.reshape(slot_count, SHIFTS, class_count)
    scores = lax.psum(partial_scores, "vol")
    squares = scores * scores
    mean_square = jnp.mean(squares, axis=(1, 2), keepdims=True)
    weights = (squares / (mean_square + EPS_W)).astype(jnp.bfloat16)
    weighted = lax.dot_general(
        weights.reshape(slot_count, SHIFTS * class_count),
        arrived,
        (((0,), (0,)), ((), ())),
        preferred_element_type=jnp.float32,
    )
    weighted = weighted.reshape(SHIFTS, class_count, quarter_rows, IMG)
    aligned = jnp.roll(weighted[0], -(SHIFTS // 2), axis=2)
    for shift_id in range(1, SHIFTS):
        aligned = aligned + jnp.roll(weighted[shift_id], shift_id - SHIFTS // 2, axis=2)
    column_ids = jnp.arange(pix_quarter, dtype=jnp.int32) % IMG
    placed = interp_index + 2 * VBOX * PLANES * column_ids[None, :]
    slab_part = jax.ops.segment_sum(aligned.reshape(-1), placed.reshape(-1), num_segments=VOXS)
    piece_len = VOXS // (n_half * n_cls)
    slab_part = jnp.transpose(slab_part.reshape(n_half, n_cls, piece_len), (1, 0, 2)).reshape(-1)
    block_len = VOXS // n_cls
    slab_full = lax.psum(slab_part, "cls")
    own_block = lax.dynamic_slice_in_dim(slab_full, lax.axis_index("cls") * block_len, block_len)
    half_id = lax.axis_index("half")
    own_piece = lax.dynamic_slice_in_dim(own_block, half_id * piece_len, piece_len)
    other_piece = lax.dynamic_slice_in_dim(own_block, (1 - half_id) * piece_len, piece_len)
    mirror_piece = partner(other_piece, "half", 0)
    first = jnp.where(half_id == 0, own_piece, mirror_piece)
    second = jnp.where(half_id == 0, mirror_piece, own_piece)
    shell_hot = (shell_index[0][:, None] == jnp.arange(NSHELL, dtype=jnp.int32)[None, :]).astype(
        jnp.float32
    )
    stats = jnp.stack([first * first, second * second, first * second])
    shell_terms = jnp.dot(stats, shell_hot, precision=lax.Precision.HIGHEST)
    shell_sums = lax.psum(shell_terms, ("half", "cls", "vol"))
    shell_fsc = shell_sums[2] / (jnp.sqrt(shell_sums[0]) * jnp.sqrt(shell_sums[1]) + EPS_F)
    mean_sq = (jnp.sum(shell_sums[0]) + jnp.sum(shell_sums[1]) + 2.0 * jnp.sum(shell_sums[2])) / (
        4.0 * n_vol * VOXS
    )
    filter_vox = jnp.dot(shell_hot, shell_fsc, precision=lax.Precision.HIGHEST)
    volume = filter_vox * (0.5 * (first + second)) / jnp.sqrt(mean_sq + EPS_F)
    return (volume[None, :], shell_fsc)


def solution(mesh):
    placed = (
        P(("half", "cls"), "vol"),
        P(("half", "cls"), None),
        P("cls", "vol"),
        P("cls", "vol"),
        P("vol", ("half", "cls")),
    )
    return jax.shard_map(
        shards,
        mesh=mesh,
        in_specs=placed,
        out_specs=(P("vol", ("half", "cls")), P()),
        check_vma=False,
    )
```

profile of v0, /device:TPU:1, one launch (start us, length us, event | category | flops | bytes accessed | tf_op | source)
XLA Modules:
  0.0 1277.2 jit_solution(14044876211775641448)
XLA Ops:
  7.2 0.8 fusion.7
  8.2 0.8 select_reduce_fusion.1
  10.1 1.8 gather_fusion
  11.9 2.2 gather.7
  14.3 3.7 select_select_fusion
  18.0 19.2 %all-to-all-start = ((bf16[64,4,4096]{2,1,0:T(4,128)(2,1)}), bf16[64,4,4096]{2,1,0:T(4,128)(2,1)S(1)}, u32[]{:S(2)}, u32[]{:S(2)}) async-start(bf16[64,4,4096]{2,1,0:T(4,128)(2,1)} %select_select_fusion), calls=%async_computation | async-start | bytes 4194304 | tf_op jit(solution)/shard_map/all_to_all | solution.py:40
  38.6 0.8 bitcast_dynamic-update-slice_fusion.3
  39.4 0.8 bitcast_dynamic-update-slice_fusion.2
  40.2 0.7 constant_dynamic-update-slice_fusion
  40.9 0.8 bitcast_dynamic-update-slice_fusion.1
  41.7 0.8 bitcast_dynamic-update-slice_fusion
  42.5 89.8 %all-to-all-done = bf16[64,4,4096]{2,1,0:T(4,128)(2,1)S(1)} async-done(((bf16[64,4,4096]{2,1,0:T(4,128)(2,1)}), bf16[64,4,4096]{2,1,0:T(4,128)(2,1)S(1)}, u32[]{:S(2)}, u32[]{:S(2)}) %all-to-all-start) | async-done | bytes 2097184 | tf_op jit(solution)/shard_map/all_to_all | solution.py:40
  132.3 2.1 reshape.142
  134.4 3.5 fusion.25
  137.9 1.1 add_bitcast_fusion
  139.0 0.9 copy.9
  139.9 2.1 reshape.116
  142.0 48.2 %all-reduce.3.cloned.1.call-done = f32[256,5,32]{0,2,1:T(8,128)} async-done(((f32[256,5,32]{0,2,1:T(8,128)}), f32[256,5,32]{0,2,1:T(8,128)}) %all-reduce.3.cloned.1.call-update) | async-done | bytes 163856 | tf_op jit(solution)/shard_map/psum | solution.py:63
  190.2 1.0 multiply_reduce_fusion
  191.1 0.9 divide_convert_fusion
  192.1 2.1 fusion.26
  196.6 683.3 %scatter_custom_fusion = f32[262144]{0:T(1024)S(1)} fusion(s32[131072]{0:T(1024)} %bitcast.88, f32[131072]{0:T(1024)S(1)} %add_add_fusion, f32[]{:T(128)} %constant.70.clone.1), kind=kCustom, calls=%fused_computation.17 | custom fusion | flops 131072 | bytes 1049088 | tf_op jit(solution)/shard_map/scatter-add | solution.py:79
  880.1 0.8 copy.26
  880.9 1.1 copy.20
  882.1 268.6 %all-reduce.5.cloned.1.call-done = f32[262144]{0:T(1024)} async-done(((f32[262144]{0:T(1024)}), f32[262144]{0:T(1024)}) %all-reduce.5.cloned.1.call-update) | async-done | bytes 1048592 | tf_op jit(solution)/shard_map/psum | solution.py:83
  1150.7 0.8 dynamic_slice.14
  1151.5 12.6 collective-permute-start
  1164.1 0.8 collective-permute-done
  1164.9 0.8 fusion.20
  1166.2 100.2 %psum.23 = f32[3,128]{1,0:T(4,128)S(1)} all-reduce(f32[3,128]{1,0:T(4,128)S(1)} %fusion.1), channel_id=1, replica_groups=mesh['half'=2,'cls'=64,'vol'=4] {'half','cls','vol'}, use_global_device_ids=true, to_apply=%region_8.9 | all-reduce | flops 384 | bytes 3072 | tf_op jit(solution)/shard_map/psum | solution.py:96
  1266.4 0.7 slice_reduce_fusion.2
  1269.1 0.7 fusion
  (48 shorter events, 6.4 us)
Async XLA Ops:
  7.2 2.9 copy-start
  18.0 19.3 %copy-start.1 = (bf16[32,4096]{1,0:T(8,128)(2,1)S(1)}, bf16[32,4096]{1,0:T(8,128)(2,1)}, u32[]{:S(2)}) copy-start(bf16[32,4096]{1,0:T(8,128)(2,1)} %param.7) | copy-start | bytes 786436
  18.0 114.3 %all-to-all-start = ((bf16[64,4,4096]{2,1,0:T(4,128)(2,1)}), bf16[64,4,4096]{2,1,0:T(4,128)(2,1)S(1)}, u32[]{:S(2)}, u32[]{:S(2)}) async-start(bf16[64,4,4096]{2,1,0:T(4,128)(2,1)} %select_select_fusion), calls=%async_computation | async-start | bytes 4194304 | tf_op jit(solution)/shard_map/all_to_all | solution.py:40
  37.3 152.9 %all-reduce.3.cloned.1.call-start = ((), (), s32[]{:S(2)}) async-start(), calls=%async_computation.1 | async-start | bytes 327680 | tf_op jit(solution)/shard_map/psum | solution.py:63
  137.9 1012.8 %all-reduce.5.cloned.1.call-start = ((), (), s32[]{:S(2)}) async-start(), calls=%async_computation.2 | async-start | bytes 2097152 | tf_op jit(solution)/shard_map/psum | solution.py:83
  880.9 284.8 %copy-start.3 = (s32[1,2048]{1,0:T(1,128)S(1)}, s32[1,2048]{1,0:T(1,128)}, u32[]{:S(2)}) copy-start(s32[1,2048]{1,0:T(1,128)} %param.9) | copy-start | bytes 24580
  1151.5 13.4 %collective-permute-start = (f32[2048]{0:T(1024)S(1)}, f32[2048]{0:T(1024)S(1)}, u32[]{:S(2)}, u32[]{:S(2)}) collective-permute-start(f32[2048]{0:T(1024)S(1)} %dynamic_slice.14), channel_id=1, source_target_pairs={{0,256},{256,0},{1,257},{257,1},{2,258},{258,2},{3,259},{259,3},{4... | collective-permute-start | bytes 24584 | tf_op jit(solution)/shard_map/ppermute | solution.py:17
  1267.1 3.3 copy-start.2
Sparse Core Ops, SparseCore 0:
  138.0 52.1 all-reduce.2
  882.2 268.4 all-reduce.4
where the time goes:
time: 1280 us
  other arithmetic  696 us (54%)
  waiting for transfers between devices  407 us (32%)
  blocking collectives  100 us (8%)
  starting transfers between devices  31.9 us (2%)
  local copies, waits for them, and re-layouts  18.2 us (1%)
  between operations  16.3 us (1%)
    scatter-add x1, other arithmetic, shards(): jax.ops.segment_sum(aligned.reshape(-1), placed.reshape(-1), num_segments...  683 us
    psum x1, waiting for transfers between devices, shards(): slab_full = lax.psum(slab_part, 'cls')  269 us
    psum x1, blocking collectives, shards(): shell_sums = lax.psum(shell_terms, ('half', 'cls', 'vol'))  100 us
    all_to_all x1, waiting for transfers between devices, shards(): lax.all_to_all(outgoing.reshape(n_cls, capacity, pix_quarter), 'cls', spl...  89.8 us
    psum x1, waiting for transfers between devices, shards(): scores = lax.psum(partial_scores, 'vol')  48.2 us
  transfers between devices with their start and end apart: 4, of which 4 were waited for; matrix products, arithmetic and copies ran while one was open for 1% of the time, Pallas kernels for 0%

commit v1 on v0

--- a/solution.py
+++ b/solution.py
@@ -60,7 +60,8 @@
         arrived, rolled_refs, (((1,), (1,)), ((), ())), preferred_element_type=jnp.float32
     )
     partial_scores = partial_scores.reshape(slot_count, SHIFTS, class_count)
-    scores = lax.psum(partial_scores, "vol")
+    terms = lax.all_gather(partial_scores, "vol", axis=0, tiled=False)
+    scores = terms.sum(axis=0)
     squares = scores * scores
     mean_square = jnp.mean(squares, axis=(1, 2), keepdims=True)
     weights = (squares / (mean_square + EPS_W)).astype(jnp.bfloat16)

time: 1280 us -> 1240 us (0.969)
  waiting for transfers between devices: 407 us -> 354 us
    psum x1 -> x0, waiting for transfers between devices: 48.2 us -> none  [shards(): scores = lax.psum(partial_scores, 'vol')]
  transfers between devices with their start and end apart: 4 -> 3, of which waited for: 4 -> 3; matrix products, arithmetic and copies ran while one was open for 1% -> 1% of each run, Pallas kernels for 0% -> 0%
where the time goes in v1:
time: 1240 us
  other arithmetic  696 us (56%)
  waiting for transfers between devices  354 us (29%)
  blocking collectives  112 us (9%)
  starting transfers between devices  31.8 us (3%)
  local copies, waits for them, and re-layouts  20.5 us (2%)
  between operations  16.3 us (1%)
    scatter-add x1, other arithmetic, shards(): jax.ops.segment_sum(aligned.reshape(-1), placed.reshape(-1), num_segments...  683 us
    psum x1, waiting for transfers between devices, shards(): slab_full = lax.psum(slab_part, 'cls')  266 us
    psum x1, blocking collectives, shards(): shell_sums = lax.psum(shell_terms, ('half', 'cls', 'vol'))  100 us
    all_to_all x1, waiting for transfers between devices, shards(): lax.all_to_all(outgoing.reshape(n_cls, capacity, pix_quarter), 'cls', spl...  87.8 us
  transfers between devices with their start and end apart: 3, of which 3 were waited for; matrix products, arithmetic and copies ran while one was open for 1% of the time, Pallas kernels for 0%

profile of v1, /device:TPU:1, one launch (start us, length us, event | category | flops | bytes accessed | tf_op | source)
XLA Modules:
  0.0 1236.8 jit_solution(1766931139198883164)
XLA Ops:
  7.2 0.8 fusion.7
  8.2 0.8 select_reduce_fusion.1
  10.1 1.8 gather_fusion
  11.9 2.2 gather.7
  14.3 3.7 select_select_fusion
  18.0 19.2 %all-to-all-start = ((bf16[64,4,4096]{2,1,0:T(4,128)(2,1)}), bf16[64,4,4096]{2,1,0:T(4,128)(2,1)S(1)}, u32[]{:S(2)}, u32[]{:S(2)}) async-start(bf16[64,4,4096]{2,1,0:T(4,128)(2,1)} %select_select_fusion), calls=%async_computation | async-start | bytes 4194304 | tf_op jit(solution)/shard_map/all_to_all | solution.py:40
  37.4 1.1 add_bitcast_fusion
  38.5 0.9 copy.9
  40.6 0.8 bitcast_dynamic-update-slice_fusion.3
  41.4 0.8 bitcast_dynamic-update-slice_fusion.2
  42.2 0.7 constant_dynamic-update-slice_fusion
  42.9 0.8 bitcast_dynamic-update-slice_fusion.1
  43.7 0.8 bitcast_dynamic-update-slice_fusion
  44.5 87.8 %all-to-all-done = bf16[64,4,4096]{2,1,0:T(4,128)(2,1)S(1)} async-done(((bf16[64,4,4096]{2,1,0:T(4,128)(2,1)}), bf16[64,4,4096]{2,1,0:T(4,128)(2,1)S(1)}, u32[]{:S(2)}, u32[]{:S(2)}) %all-to-all-start) | async-done | bytes 2097184 | tf_op jit(solution)/shard_map/all_to_all | solution.py:40
  132.3 2.1 reshape.169
  134.4 2.8 fusion.25
  137.2 11.4 all-gather
  148.6 2.2 reshape.167
  150.8 1.5 reduce_sum.71
  152.4 2.1 reshape.143
  154.4 2.1 fusion.26
  159.0 683.5 %scatter_custom_fusion = f32[262144]{0:T(1024)S(1)} fusion(s32[131072]{0:T(1024)} %bitcast.90, f32[131072]{0:T(1024)S(1)} %add_add_fusion, f32[]{:T(128)} %constant.70.clone.1), kind=kCustom, calls=%fused_computation.17 | custom fusion | flops 131072 | bytes 1049088 | tf_op jit(solution)/shard_map/scatter-add | solution.py:80
  842.6 0.8 copy.26
  843.5 1.1 copy.20
  844.6 265.6 %all-reduce.2.cloned.1.call-done = f32[262144]{0:T(1024)} async-done(((f32[262144]{0:T(1024)}), f32[262144]{0:T(1024)}) %all-reduce.2.cloned.1.call-update) | async-done | bytes 1048592 | tf_op jit(solution)/shard_map/psum | solution.py:84
  1110.2 0.8 dynamic_slice.14
  1111.0 12.6 %collective-permute-start = (f32[2048]{0:T(1024)S(1)}, f32[2048]{0:T(1024)S(1)}, u32[]{:S(2)}, u32[]{:S(2)}) collective-permute-start(f32[2048]{0:T(1024)S(1)} %dynamic_slice.14), channel_id=1, source_target_pairs={{0,256},{256,0},{1,257},{257,1},{2,258},{258,2},{3,259},{259,3},{4... | collective-permute-start | bytes 24584 | tf_op jit(solution)/shard_map/ppermute | solution.py:17
  1123.6 0.8 collective-permute-done
  1124.4 0.8 fusion.20
  1125.7 100.2 %psum.15 = f32[3,128]{1,0:T(4,128)S(1)} all-reduce(f32[3,128]{1,0:T(4,128)S(1)} %fusion.1), channel_id=1, replica_groups=mesh['half'=2,'cls'=64,'vol'=4] {'half','cls','vol'}, use_global_device_ids=true, to_apply=%region_8.9 | all-reduce | flops 384 | bytes 3072 | tf_op jit(solution)/shard_map/psum | solution.py:97
  1225.9 0.7 slice_reduce_fusion.2
  1228.6 0.7 fusion
  (48 shorter events, 6.4 us)
Async XLA Ops:
  7.2 2.9 copy-start
  18.0 19.3 %copy-start.1 = (bf16[32,4096]{1,0:T(8,128)(2,1)S(1)}, bf16[32,4096]{1,0:T(8,128)(2,1)}, u32[]{:S(2)}) copy-start(bf16[32,4096]{1,0:T(8,128)(2,1)} %param.7) | copy-start | bytes 786436
  18.0 114.3 %all-to-all-start = ((bf16[64,4,4096]{2,1,0:T(4,128)(2,1)}), bf16[64,4,4096]{2,1,0:T(4,128)(2,1)S(1)}, u32[]{:S(2)}, u32[]{:S(2)}) async-start(bf16[64,4,4096]{2,1,0:T(4,128)(2,1)} %select_select_fusion), calls=%async_computation | async-start | bytes 4194304 | tf_op jit(solution)/shard_map/all_to_all | solution.py:40
  37.3 1072.9 %all-reduce.2.cloned.1.call-start = ((), (), s32[]{:S(2)}) async-start(), calls=%async_computation.1 | async-start | bytes 2097152 | tf_op jit(solution)/shard_map/psum | solution.py:84
  843.5 281.7 %copy-start.3 = (s32[1,2048]{1,0:T(1,128)S(1)}, s32[1,2048]{1,0:T(1,128)}, u32[]{:S(2)}) copy-start(s32[1,2048]{1,0:T(1,128)} %param.9) | copy-start | bytes 24580
  1111.0 13.4 %collective-permute-start = (f32[2048]{0:T(1024)S(1)}, f32[2048]{0:T(1024)S(1)}, u32[]{:S(2)}, u32[]{:S(2)}) collective-permute-start(f32[2048]{0:T(1024)S(1)} %dynamic_slice.14), channel_id=1, source_target_pairs={{0,256},{256,0},{1,257},{257,1},{2,258},{258,2},{3,259},{259,3},{4... | collective-permute-start | bytes 24584 | tf_op jit(solution)/shard_map/ppermute | solution.py:17
  1226.6 3.3 copy-start.2
Sparse Core Ops, SparseCore 0:
  844.7 265.4 all-reduce.1
